TPU v7x, 32 devices: a whole 2x2x4 slice. The times are simulated.
32 devices in a mesh: ox: 8 (over z, x), oy: 4 (over y, core).
Axes of the slice: x: 2, y: 2, z: 4, core: 2. Of those that a mesh axis runs over, the one named last changes fastest.
Arguments:
- atm_flux: bfloat16 [4, 40, 1024], P(None, 'oy', 'ox'), may hold values from -6 to 6
- remap_weights: bfloat16 [128, 12, 128, 128], P('ox', 'oy'), may hold values from -0.3125 to 0.3125
- tile_slots: int32 [128, 12], P('ox', 'oy'), may hold values from 0 to 23, as said below
- need_blocks: int32 [64, 12], P('ox', 'oy'), may hold values from -1 to 9, as said below
- send_blocks: int32 [64, 12], P('ox', 'oy'), may hold values from -1 to 9, as said below
- ocean_state: float32 [4, 16, 128, 512], P(None, None, 'ox', 'oy'), may hold values from -6 to 6
- land_mask: int32 [128, 512], P('ox', 'oy'), may hold values 0 or 1
- diffusivity: float32 [16], replicated, may hold values from 0.02 to 0.2
Outputs:
- ocean_final: float32 [4, 16, 128, 512], P(None, None, 'ox', 'oy')
- atmos_surface: float32 [40, 1024], P('oy', 'ox')
Inputs may be any that keep to these rules, and one draw needn't show every extreme that they name: `tile_slots`: entry [x, j * 3 + k] is q * 3 + s: the s-th block that owner q sends the ocean device of row x and latitude group j, with s below the number of blocks that owner sends it. `need_blocks`: entry [i * 8 + q, j * 3 + s] is the local block of owner (q, j) that ocean device (i, j) takes in place s, or -1; the first 1 to 3 places hold distinct blocks and the rest -1; every ocean device takes 3 blocks from some owner, and some device takes 3 from every owner. `send_blocks`: entry [q * 8 + i, j * 3 + s] equals need_blocks[i * 8 + q, j * 3 + s].
All inputs are finite; a program needn't handle non-finite values. No bound on the sum of `land_mask` on one device may be relied on, other than what follows from the above.
Results may differ from a plain program's by a relative error of at most 0.0022.
Values may be sent and summed in bfloat16 or wider, within the bound.
No kernel may reach another device: no remote copies, remote signals or barrier semaphores. Data moves between devices by JAX's collectives and lax.ppermute only.
A program may use at most 64 MiB of HBM per device.

v0:
```python
import jax
import jax.numpy as jnp
from jax import lax
from jax.sharding import PartitionSpec as P

STEPS = 3
advect_coef = 0.25
pressure_coef = 0.1
thermal_coef = 0.2
haline_coef = 0.8
coriolis_coef = 0.5
vertical_coef = 0.1
forcing_coef = 0.5


def with_halo(block, sides, width):
    for axis, dim in sides:
        count = lax.axis_size(axis)
        forward = [(i, i + 1) for i in range(count - 1)]
        backward = [(target, source) for source, target in forward]
        low = lax.ppermute(
            lax.slice_in_dim(block, block.shape[dim] - width, None, axis=dim), axis, forward
        )
        high = lax.ppermute(lax.slice_in_dim(block, 0, width, axis=dim), axis, backward)
        block = jnp.concatenate([low, block, high], axis=dim)
    return block


def advance(padded, center, diffusivity, coriolis, forcing, wetness):
    east = padded[:, :, 2:, 1:-1]
    west = padded[:, :, :-2, 1:-1]
    north = padded[:, :, 1:-1, 2:]
    south = padded[:, :, 1:-1, :-2]
    zonal = center[0]
    meridional = center[1]
    advection = (
        -advect_coef * 0.5 * (zonal[None] * (east - west) + meridional[None] * (north - south))
    )
    laplace = diffusivity[None, :, None, None] * (east + west + north + south - 4.0 * center)
    upper = jnp.concatenate([center[:, :1], center[:, :-1]], axis=1)
    lower = jnp.concatenate([center[:, 1:], center[:, -1:]], axis=1)
    mixing = vertical_coef * (upper + lower - 2.0 * center)
    density = haline_coef * padded[3] - thermal_coef * padded[2]
    pressure = jnp.cumsum(density, axis=0) - 0.5 * density
    grad_east = pressure[:, 2:, 1:-1] - pressure[:, :-2, 1:-1]
    grad_north = pressure[:, 1:-1, 2:] - pressure[:, 1:-1, :-2]
    zonal_push = coriolis * meridional - pressure_coef * 0.5 * grad_east
    merid_push = -coriolis * zonal - pressure_coef * 0.5 * grad_north
    tracer_zero = jnp.zeros((2,) + zonal.shape, jnp.float32)
    momentum = jnp.concatenate([zonal_push[None], merid_push[None], tracer_zero], axis=0)
    total = advection + laplace + mixing + momentum
    total = total.at[:, 0].add(forcing_coef * forcing)
    return center + wetness * total


def row_targets(tile_slots, need_blocks, capacity, owners):
    owner_of = tile_slots // capacity
    place_of = tile_slots % capacity
    return need_blocks[owner_of, place_of] * owners + owner_of


def lat_factor(first_cell, count, lat_total):
    latitude = (first_cell + jnp.arange(count, dtype=jnp.int32)).astype(jnp.float32)
    return coriolis_coef * (2.0 * (latitude + 0.5) / lat_total - 1.0)


def per_device(
    atm_flux,
    remap_weights,
    tile_slots,
    need_blocks,
    send_blocks,
    ocean_state,
    land_mask,
    diffusivity,
):
    flux_fields = atm_flux.shape[0]
    blocks_here = atm_flux.shape[1]
    block_width = atm_flux.shape[2]
    owners = lax.axis_size("ox")
    tile_count = tile_slots.shape[0]
    refs_tile = tile_slots.shape[1]
    capacity = send_blocks.shape[1]
    whole = lax.all_gather(atm_flux, "ox", axis=2, tiled=True)
    table = whole.reshape(flux_fields, blocks_here * owners, block_width)
    picks = table[:, row_targets(tile_slots, need_blocks, capacity, owners)]
    forcing = jnp.einsum("ftka,tkra->ftr", picks, remap_weights, preferred_element_type=jnp.float32)
    lat_cells = ocean_state.shape[3]
    lat_total = lat_cells * lax.axis_size("oy")
    lat_start = lax.axis_index("oy") * lat_cells
    wetness = land_mask.astype(jnp.float32)
    state = ocean_state
    coriolis = lat_factor(lat_start, lat_cells, lat_total)
    for repeat in range(STEPS):
        padded = with_halo(state, (("ox", 2), ("oy", 3)), 1)
        state = advance(padded, state, diffusivity, coriolis, forcing, wetness)
    surface = state[2, 0].astype(jnp.bfloat16)
    pieces = jnp.einsum("tkra,tr->tka", remap_weights, surface, preferred_element_type=jnp.float32)
    pieces = pieces.reshape(tile_count * refs_tile, block_width)
    targets = row_targets(tile_slots, need_blocks, capacity, owners).reshape(-1)
    segment_line = jnp.arange(blocks_here * owners, dtype=jnp.int32)
    select = (targets[:, None] == segment_line[None, :]).astype(jnp.float32)
    dense = lax.dot_general(
        select, pieces, (((0,), (0,)), ((), ())), precision=lax.Precision.HIGHEST
    )
    dense = dense.reshape(blocks_here, owners * block_width)
    atmos_surface = lax.psum_scatter(dense, "ox", scatter_dimension=1, tiled=True)
    return (state, atmos_surface)


def solution(mesh):
    return jax.shard_map(
        per_device,
        mesh=mesh,
        in_specs=(
            P(None, "oy", "ox"),
            P("ox", "oy", None, None),
            P("ox", "oy"),
            P("ox", "oy"),
            P("ox", "oy"),
            P(None, None, "ox", "oy"),
            P("ox", "oy"),
            P(),
        ),
        out_specs=(P(None, None, "ox", "oy"), P("oy", "ox")),
        check_vma=False,
    )
```

profile of v0, /device:TPU:0, one launch (start us, length us, event | category | flops | bytes accessed | tf_op | source)
XLA Modules:
  0.0 182.9 jit_solution(17034254981242002225)
XLA Ops:
  7.2 1.2 fusion.83
  8.4 4.8 %collective-permute-start.1 = (f32[4,16,1,128]{3,2,1,0:T(1,128)S(1)}, f32[4,16,1,128]{3,2,1,0:T(1,128)S(1)}, u32[]{:S(2)}, u32[]{:S(2)}) collective-permute-start(f32[4,16,1,128]{3,2,1,0:T(1,128)S(1)} %get-tuple-element.76), channel_id=1, source_target_pairs={{0,4},{4,8},{8,12},{12,16},{16,20},{20,24},{24,28},{1,5},{5,9},{9,... | collective-permute-start | bytes 98312 | tf_op jit(solution)/shard_map/ppermute | solution.py:21
  13.3 1.3 collective-permute-start
  14.6 0.8 fusion.85
  15.4 1.7 slice_bitcast_fusion.5
  17.1 2.1 %fusion.84 = (f32[4,15,16,128]{3,2,1,0:T(8,128)S(1)}, f32[4,15,16,128]{3,2,1,0:T(8,128)}) fusion(f32[4,16,16,128]{3,2,1,0:T(8,128)} %param.18), kind=kLoop, calls=%fused_computation.163 | loop fusion | bytes 1966080 | tf_op jit(solution)/shard_map/slice | solution.py:41
  19.4 1.1 gather_fusion
  20.7 22.4 %all_gather.3 = bf16[4,10,1024]{2,0,1:T(4,128)(2,1)S(1)} all-gather(bf16[4,10,128]{2,0,1:T(4,128)(2,1)S(1)} %copy-done.16), channel_id=1, replica_groups=mesh['ox'=8,'oy'=4] {'ox'}, dimensions={2}, use_global_device_ids=true | all-gather | bytes 92160 | tf_op jit(solution)/shard_map/all_gather | solution.py:84
  43.0 0.6 gather_fusion.1
  43.7 0.6 convolution_bitcast_fusion
  44.5 1.2 fusion.76
  45.7 2.2 %copy.144 = f32[4,16,18,1]{2,1,3,0:T(8,128)} copy(f32[4,16,18,1]{3,2,1,0:T(8,128)} %get-tuple-element.56) | data formatting | bytes 9216 | tf_op jit(solution)/shard_map/slice | solution.py:22
  47.9 1.1 copy.142
  49.0 1.3 collective-permute-start.2
  50.2 3.6 %collective-permute-start.3 = (f32[4,16,18,1]{2,1,3,0:T(8,128)}, f32[4,16,18,1]{2,1,3,0:T(8,128)}, u32[]{:S(2)}, u32[]{:S(2)}) collective-permute-start(f32[4,16,18,1]{2,1,3,0:T(8,128)} %copy.144), channel_id=1, source_target_pairs={{0,1},{1,2},{2,3},{4,5},{5,6},{6,7},{8,9},{9,10},{10,11},{12,13},{... | collective-permute-start | bytes 13832 | tf_op jit(solution)/shard_map/ppermute | solution.py:21
  53.9 0.6 add_multiply_fusion
  54.5 0.7 convert_element_type.18
  55.2 0.7 eq.18
  55.8 0.6 pad.62.clone
  56.5 1.3 copy.145
  57.7 2.1 %copy.143 = f32[4,16,18,1]{3,2,1,0:T(8,128)} copy(f32[4,16,18,1]{2,1,3,0:T(8,128)} %collective-permute-done.2) | data formatting | bytes 9216 | tf_op jit(solution)/shard_map/ppermute | solution.py:24
  59.9 2.2 %reduce-window_subtract_fusion.2 = f32[16,18,130]{2,1,0:T(8,128)S(1)} fusion(f32[4,16,18,1]{3,2,1,0:T(8,128)} %copy.143, f32[4,16,1,128]{3,2,1,0:T(1,128)S(1)} %collective-permute-done, f32[4,16,16,128]{3,2,1,0:T(8,128)S(1)} %copy-done.2, f32[4,16,1,128]{3,2,1,0:T(1,128)S(1)} %collective-permute-done.1, f32[4,16,18,1]{3,2,1,0:T(8,128)S(1)} %copy.145), kind=kOutput, calls=%fused_computation.4 | output fusion | flops 1460160 | bytes 748800 | tf_op jit(solution)/shard_map/jit(cumsum)/reduce_window_sum | solution.py:44
  62.2 0.2 fusion.47
  62.4 0.9 copy-done.4
  63.3 0.9 fusion.3
  64.3 0.9 fusion.81
  65.2 1.3 collective-permute-start.5
  66.5 1.3 collective-permute-start.4
  67.8 0.7 slice_bitcast_fusion.3
  68.5 3.8 %collective-permute-done.4 = f32[4,16,1,128]{3,2,1,0:T(1,128)S(1)} collective-permute-done((f32[4,16,1,128]{3,2,1,0:T(1,128)S(1)}, f32[4,16,1,128]{3,2,1,0:T(1,128)S(1)}, u32[]{:S(2)}, u32[]{:S(2)}) %collective-permute-start.4) | collective-permute-done | bytes 32800 | tf_op jit(solution)/shard_map/ppermute | solution.py:24
  72.4 1.2 fusion.75
  73.6 2.2 %copy.156 = f32[4,16,18,1]{2,1,3,0:T(8,128)} copy(f32[4,16,18,1]{3,2,1,0:T(8,128)} %get-tuple-element.54) | data formatting | bytes 9216 | tf_op jit(solution)/shard_map/slice | solution.py:22
  75.8 1.1 copy.154
  76.9 1.3 collective-permute-start.6
  78.2 3.6 %collective-permute-start.7 = (f32[4,16,18,1]{2,1,3,0:T(8,128)}, f32[4,16,18,1]{2,1,3,0:T(8,128)}, u32[]{:S(2)}, u32[]{:S(2)}) collective-permute-start(f32[4,16,18,1]{2,1,3,0:T(8,128)} %copy.156), channel_id=1, source_target_pairs={{0,1},{1,2},{2,3},{4,5},{5,6},{6,7},{8,9},{9,10},{10,11},{12,13},{... | collective-permute-start | bytes 13832 | tf_op jit(solution)/shard_map/ppermute | solution.py:21
  81.8 0.6 collective-permute-done.7
  82.4 1.3 copy.157
  83.6 2.1 %copy.155 = f32[4,16,18,1]{3,2,1,0:T(8,128)} copy(f32[4,16,18,1]{2,1,3,0:T(8,128)} %collective-permute-done.6) | data formatting | bytes 9216 | tf_op jit(solution)/shard_map/ppermute | solution.py:24
  85.8 2.2 %reduce-window_subtract_fusion.1 = f32[16,18,130]{2,1,0:T(8,128)S(1)} fusion(f32[4,16,18,1]{3,2,1,0:T(8,128)} %copy.155, f32[4,16,1,128]{3,2,1,0:T(1,128)S(1)} %collective-permute-done.4, f32[4,16,16,128]{3,2,1,0:T(8,128)S(1)} %multiply_add_fusion.2, f32[4,16,1,128]{3,2,1,0:T(1,128)S(1)} %collective-permute-done.5, f32[4,16,18,1]{3,2,1,0:T(8,128)S(1)} %copy.157), kind=kOutput, calls=%fused_computation.3 | output fusion | flops 1460160 | bytes 748800 | tf_op jit(solution)/shard_map/jit(cumsum)/reduce_window_sum | solution.py:44
  88.0 0.2 fusion.41
  88.3 0.9 copy-done.5
  89.2 0.9 fusion.7
  90.2 0.9 fusion.78
  91.1 3.6 %collective-permute-start.9 = (f32[4,16,1,128]{3,2,1,0:T(1,128)S(1)}, f32[4,16,1,128]{3,2,1,0:T(1,128)S(1)}, u32[]{:S(2)}, u32[]{:S(2)}) collective-permute-start(f32[4,16,1,128]{3,2,1,0:T(1,128)S(1)} %get-tuple-element.60), channel_id=1, source_target_pairs={{0,4},{4,8},{8,12},{12,16},{16,20},{20,24},{24,28},{1,5},{5,9},{9,... | collective-permute-start | bytes 98312 | tf_op jit(solution)/shard_map/ppermute | solution.py:21
  94.7 1.3 collective-permute-start.8
  96.0 0.7 slice_bitcast_fusion.1
  96.7 4.1 %collective-permute-done.8 = f32[4,16,1,128]{3,2,1,0:T(1,128)S(1)} collective-permute-done((f32[4,16,1,128]{3,2,1,0:T(1,128)S(1)}, f32[4,16,1,128]{3,2,1,0:T(1,128)S(1)}, u32[]{:S(2)}, u32[]{:S(2)}) %collective-permute-start.8) | collective-permute-done | bytes 32800 | tf_op jit(solution)/shard_map/ppermute | solution.py:24
  101.0 1.2 fusion.74
  102.2 2.2 %copy.162 = f32[4,16,18,1]{2,1,3,0:T(8,128)} copy(f32[4,16,18,1]{3,2,1,0:T(8,128)} %get-tuple-element.52) | data formatting | bytes 9216 | tf_op jit(solution)/shard_map/slice | solution.py:22
  104.4 1.1 copy.160
  105.5 1.3 collective-permute-start.10
  106.7 3.6 %collective-permute-start.11 = (f32[4,16,18,1]{2,1,3,0:T(8,128)}, f32[4,16,18,1]{2,1,3,0:T(8,128)}, u32[]{:S(2)}, u32[]{:S(2)}) collective-permute-start(f32[4,16,18,1]{2,1,3,0:T(8,128)} %copy.162), channel_id=1, source_target_pairs={{0,1},{1,2},{2,3},{4,5},{5,6},{6,7},{8,9},{9,10},{10,11},{12,13},{... | collective-permute-start | bytes 13832 | tf_op jit(solution)/shard_map/ppermute | solution.py:21
  110.4 0.6 collective-permute-done.11
  111.0 1.3 copy.163
  112.2 2.1 %copy.161 = f32[4,16,18,1]{3,2,1,0:T(8,128)} copy(f32[4,16,18,1]{2,1,3,0:T(8,128)} %collective-permute-done.10) | data formatting | bytes 9216 | tf_op jit(solution)/shard_map/ppermute | solution.py:24
  114.4 2.2 %reduce-window_subtract_fusion = f32[16,18,130]{2,1,0:T(8,128)S(1)} fusion(f32[4,16,18,1]{3,2,1,0:T(8,128)} %copy.161, f32[4,16,1,128]{3,2,1,0:T(1,128)S(1)} %collective-permute-done.8, f32[4,16,16,128]{3,2,1,0:T(8,128)S(1)} %multiply_add_fusion.1, f32[4,16,1,128]{3,2,1,0:T(1,128)S(1)} %collective-permute-done.9, f32[4,16,18,1]{3,2,1,0:T(8,128)S(1)} %copy.163), kind=kOutput, calls=%fused_computation.2 | output fusion | flops 1460160 | bytes 748800 | tf_op jit(solution)/shard_map/jit(cumsum)/reduce_window_sum | solution.py:44
  116.6 0.2 fusion.35
  116.9 0.9 copy-done.3
  117.8 0.9 fusion.11
  118.8 0.4 fusion.58
  119.2 0.1 copy-done.25
  119.3 0.3 fusion.51
  119.6 0.7 reshape.143
  120.3 55.7 %reduce-scatter.2.cloned.1.call-done = f32[10,128]{1,0:T(8,128)} async-done(((f32[10,1024]{1,0:T(8,128)}), f32[10,128]{1,0:T(8,128)}) %reduce-scatter.2.cloned.1.call-update) | async-done | bytes 5136 | tf_op jit(solution)/shard_map/reduce_scatter | solution.py:107
  (85 shorter events, 1.3 us)
Async XLA Ops:
  7.2 36.5 %copy-start = (bf16[16,3,128,128]{3,2,1,0:T(8,128)(2,1)S(1)}, bf16[16,3,128,128]{3,2,1,0:T(8,128)(2,1)}, u32[]{:S(2)}) copy-start(bf16[16,3,128,128]{3,2,1,0:T(8,128)(2,1)} %param.15) | copy-start | bytes 4718596
  7.2 12.0 %copy-start.26 = (s32[16,3]{0,1:T(4,128)S(1)}, s32[16,3]{0,1:T(4,128)}, u32[]{:S(2)}) copy-start(s32[16,3]{0,1:T(4,128)} %param.16) | copy-start | bytes 580
  7.2 12.2 %copy-start.1 = (s32[8,3]{0,1:T(4,128)S(1)}, s32[8,3]{0,1:T(4,128)}, u32[]{:S(2)}) copy-start(s32[8,3]{0,1:T(4,128)} %param.17) | copy-start | bytes 292
  7.2 168.8 %reduce-scatter.2.cloned.1.call-start = ((), (), s32[]{:S(2)}) async-start(), calls=%async_computation.1 | async-start | bytes 73728 | tf_op jit(solution)/shard_map/reduce_scatter | solution.py:107
  8.4 35.9 %collective-permute-start.1 = (f32[4,16,1,128]{3,2,1,0:T(1,128)S(1)}, f32[4,16,1,128]{3,2,1,0:T(1,128)S(1)}, u32[]{:S(2)}, u32[]{:S(2)}) collective-permute-start(f32[4,16,1,128]{3,2,1,0:T(1,128)S(1)} %get-tuple-element.76), channel_id=1, source_target_pairs={{0,4},{4,8},{8,12},{12,16},{16,20},{20,24},{24,28},{1,5},{5,9},{9,... | collective-permute-start | bytes 98312 | tf_op jit(solution)/shard_map/ppermute | solution.py:21
  13.3 31.0 %collective-permute-start = (f32[4,16,1,128]{3,2,1,0:T(1,128)S(1)}, f32[4,16,1,128]{3,2,1,0:T(1,128)S(1)}, u32[]{:S(2)}, u32[]{:S(2)}) collective-permute-start(f32[4,16,1,128]{3,2,1,0:T(1,128)S(1)} %get-tuple-element.77), channel_id=1, source_target_pairs={{4,0},{8,4},{12,8},{16,12},{20,16},{24,20},{28,24},{5,1},{9,5},{13... | collective-permute-start | bytes 98312 | tf_op jit(solution)/shard_map/ppermute | solution.py:24
  19.4 1.3 copy-start.16
  20.4 23.9 %copy-start.2 = (f32[4,16,16,128]{3,2,1,0:T(8,128)S(1)}, f32[4,16,16,128]{3,2,1,0:T(8,128)}, u32[]{:S(2)}) copy-start(f32[4,16,16,128]{3,2,1,0:T(8,128)} %param.18) | copy-start | bytes 1572868
  49.0 8.8 %collective-permute-start.2 = (f32[4,16,18,1]{2,1,3,0:T(8,128)}, f32[4,16,18,1]{2,1,3,0:T(8,128)}, u32[]{:S(2)}, u32[]{:S(2)}) collective-permute-start(f32[4,16,18,1]{2,1,3,0:T(8,128)} %copy.142), channel_id=1, source_target_pairs={{1,0},{2,1},{3,2},{5,4},{6,5},{7,6},{9,8},{10,9},{11,10},{13,12},{... | collective-permute-start | bytes 13832 | tf_op jit(solution)/shard_map/ppermute | solution.py:24
  50.2 6.2 %collective-permute-start.3 = (f32[4,16,18,1]{2,1,3,0:T(8,128)}, f32[4,16,18,1]{2,1,3,0:T(8,128)}, u32[]{:S(2)}, u32[]{:S(2)}) collective-permute-start(f32[4,16,18,1]{2,1,3,0:T(8,128)} %copy.144), channel_id=1, source_target_pairs={{0,1},{1,2},{2,3},{4,5},{5,6},{6,7},{8,9},{9,10},{10,11},{12,13},{... | collective-permute-start | bytes 13832 | tf_op jit(solution)/shard_map/ppermute | solution.py:21
  59.9 2.3 %copy-start.17 = (f32[128]{0:T(128)S(1)}, f32[128]{0:T(128)}, u32[]{:S(2)}) copy-start(f32[128]{0:T(128)} %get-tuple-element.82) | copy-start | bytes 1540
  59.9 2.3 %copy-start.18 = (f32[128]{0:T(128)S(1)}, f32[128]{0:T(128)}, u32[]{:S(2)}) copy-start(f32[128]{0:T(128)} %get-tuple-element.83) | copy-start | bytes 1540
  59.9 2.5 %copy-start.6 = (f32[4,15,16,128]{3,2,1,0:T(8,128)S(1)}, f32[4,15,16,128]{3,2,1,0:T(8,128)}, u32[]{:S(2)}) copy-start(f32[4,15,16,128]{3,2,1,0:T(8,128)} %get-tuple-element.79) | copy-start | bytes 1474564
  59.9 2.5 %copy-start.10 = (f32[16,16,128]{2,1,0:T(8,128)S(1)}, f32[16,16,128]{2,1,0:T(8,128)}, u32[]{:S(2)}) copy-start(f32[16,16,128]{2,1,0:T(8,128)} %get-tuple-element.74) | copy-start | bytes 393220
  59.9 2.5 %copy-start.11 = (f32[16,16,128]{2,1,0:T(8,128)S(1)}, f32[16,16,128]{2,1,0:T(8,128)}, u32[]{:S(2)}) copy-start(f32[16,16,128]{2,1,0:T(8,128)} %get-tuple-element.75) | copy-start | bytes 393220
  59.9 2.5 %copy-start.19 = (f32[16]{0:T(128)S(1)}, f32[16]{0:T(128)}, u32[]{:S(2)}) copy-start(f32[16]{0:T(128)} %param.20) | copy-start | bytes 196
  59.9 2.5 %copy-start.22 = (f32[4]{0:T(128)S(1)}, f32[4]{0:T(128)}, u32[]{:S(2)}) copy-start(f32[4]{0:T(128)} %pad.62.clone) | copy-start | bytes 52
  62.1 1.1 copy-start.4
  65.2 3.3 %collective-permute-start.5 = (f32[4,16,1,128]{3,2,1,0:T(1,128)S(1)}, f32[4,16,1,128]{3,2,1,0:T(1,128)S(1)}, u32[]{:S(2)}, u32[]{:S(2)}) collective-permute-start(f32[4,16,1,128]{3,2,1,0:T(1,128)S(1)} %get-tuple-element.68), channel_id=1, source_target_pairs={{0,4},{4,8},{8,12},{12,16},{16,20},{20,24},{24,28},{1,5},{5,9},{9,... | collective-permute-start | bytes 98312 | tf_op jit(solution)/shard_map/ppermute | solution.py:21
  66.5 5.8 %collective-permute-start.4 = (f32[4,16,1,128]{3,2,1,0:T(1,128)S(1)}, f32[4,16,1,128]{3,2,1,0:T(1,128)S(1)}, u32[]{:S(2)}, u32[]{:S(2)}) collective-permute-start(f32[4,16,1,128]{3,2,1,0:T(1,128)S(1)} %get-tuple-element.69), channel_id=1, source_target_pairs={{4,0},{8,4},{12,8},{16,12},{20,16},{24,20},{28,24},{5,1},{9,5},{13... | collective-permute-start | bytes 98312 | tf_op jit(solution)/shard_map/ppermute | solution.py:24
  76.9 6.8 %collective-permute-start.6 = (f32[4,16,18,1]{2,1,3,0:T(8,128)}, f32[4,16,18,1]{2,1,3,0:T(8,128)}, u32[]{:S(2)}, u32[]{:S(2)}) collective-permute-start(f32[4,16,18,1]{2,1,3,0:T(8,128)} %copy.154), channel_id=1, source_target_pairs={{1,0},{2,1},{3,2},{5,4},{6,5},{7,6},{9,8},{10,9},{11,10},{13,12},{... | collective-permute-start | bytes 13832 | tf_op jit(solution)/shard_map/ppermute | solution.py:24
  78.2 4.2 %collective-permute-start.7 = (f32[4,16,18,1]{2,1,3,0:T(8,128)}, f32[4,16,18,1]{2,1,3,0:T(8,128)}, u32[]{:S(2)}, u32[]{:S(2)}) collective-permute-start(f32[4,16,18,1]{2,1,3,0:T(8,128)} %copy.156), channel_id=1, source_target_pairs={{0,1},{1,2},{2,3},{4,5},{5,6},{6,7},{8,9},{9,10},{10,11},{12,13},{... | collective-permute-start | bytes 13832 | tf_op jit(solution)/shard_map/ppermute | solution.py:21
  85.8 2.4 %copy-start.8 = (f32[4,15,16,128]{3,2,1,0:T(8,128)S(1)}, f32[4,15,16,128]{3,2,1,0:T(8,128)}, u32[]{:S(2)}) copy-start(f32[4,15,16,128]{3,2,1,0:T(8,128)} %get-tuple-element.71) | copy-start | bytes 1474564
  85.8 2.4 %copy-start.14 = (f32[16,16,128]{2,1,0:T(8,128)S(1)}, f32[16,16,128]{2,1,0:T(8,128)}, u32[]{:S(2)}) copy-start(f32[16,16,128]{2,1,0:T(8,128)} %get-tuple-element.66) | copy-start | bytes 393220
  85.8 2.5 %copy-start.15 = (f32[16,16,128]{2,1,0:T(8,128)S(1)}, f32[16,16,128]{2,1,0:T(8,128)}, u32[]{:S(2)}) copy-start(f32[16,16,128]{2,1,0:T(8,128)} %get-tuple-element.67) | copy-start | bytes 393220
  85.8 2.5 %copy-start.20 = (f32[16]{0:T(128)S(1)}, f32[16]{0:T(128)}, u32[]{:S(2)}) copy-start(f32[16]{0:T(128)} %param.20) | copy-start | bytes 196
  85.8 2.5 %copy-start.23 = (f32[4]{0:T(128)S(1)}, f32[4]{0:T(128)}, u32[]{:S(2)}) copy-start(f32[4]{0:T(128)} %pad.62.clone) | copy-start | bytes 52
  88.0 1.1 copy-start.5
  91.1 5.7 %collective-permute-start.9 = (f32[4,16,1,128]{3,2,1,0:T(1,128)S(1)}, f32[4,16,1,128]{3,2,1,0:T(1,128)S(1)}, u32[]{:S(2)}, u32[]{:S(2)}) collective-permute-start(f32[4,16,1,128]{3,2,1,0:T(1,128)S(1)} %get-tuple-element.60), channel_id=1, source_target_pairs={{0,4},{4,8},{8,12},{12,16},{16,20},{20,24},{24,28},{1,5},{5,9},{9,... | collective-permute-start | bytes 98312 | tf_op jit(solution)/shard_map/ppermute | solution.py:21
  94.7 6.1 %collective-permute-start.8 = (f32[4,16,1,128]{3,2,1,0:T(1,128)S(1)}, f32[4,16,1,128]{3,2,1,0:T(1,128)S(1)}, u32[]{:S(2)}, u32[]{:S(2)}) collective-permute-start(f32[4,16,1,128]{3,2,1,0:T(1,128)S(1)} %get-tuple-element.61), channel_id=1, source_target_pairs={{4,0},{8,4},{12,8},{16,12},{20,16},{24,20},{28,24},{5,1},{9,5},{13... | collective-permute-start | bytes 98312 | tf_op jit(solution)/shard_map/ppermute | solution.py:24
  105.5 6.8 %collective-permute-start.10 = (f32[4,16,18,1]{2,1,3,0:T(8,128)}, f32[4,16,18,1]{2,1,3,0:T(8,128)}, u32[]{:S(2)}, u32[]{:S(2)}) collective-permute-start(f32[4,16,18,1]{2,1,3,0:T(8,128)} %copy.160), channel_id=1, source_target_pairs={{1,0},{2,1},{3,2},{5,4},{6,5},{7,6},{9,8},{10,9},{11,10},{13,12},{... | collective-permute-start | bytes 13832 | tf_op jit(solution)/shard_map/ppermute | solution.py:24
  106.7 4.2 %collective-permute-start.11 = (f32[4,16,18,1]{2,1,3,0:T(8,128)}, f32[4,16,18,1]{2,1,3,0:T(8,128)}, u32[]{:S(2)}, u32[]{:S(2)}) collective-permute-start(f32[4,16,18,1]{2,1,3,0:T(8,128)} %copy.162), channel_id=1, source_target_pairs={{0,1},{1,2},{2,3},{4,5},{5,6},{6,7},{8,9},{9,10},{10,11},{12,13},{... | collective-permute-start | bytes 13832 | tf_op jit(solution)/shard_map/ppermute | solution.py:21
  114.4 2.4 %copy-start.7 = (f32[4,15,16,128]{3,2,1,0:T(8,128)S(1)}, f32[4,15,16,128]{3,2,1,0:T(8,128)}, u32[]{:S(2)}) copy-start(f32[4,15,16,128]{3,2,1,0:T(8,128)} %get-tuple-element.63) | copy-start | bytes 1474564
  114.4 2.4 %copy-start.12 = (f32[16,16,128]{2,1,0:T(8,128)S(1)}, f32[16,16,128]{2,1,0:T(8,128)}, u32[]{:S(2)}) copy-start(f32[16,16,128]{2,1,0:T(8,128)} %get-tuple-element.58) | copy-start | bytes 393220
  114.4 2.5 %copy-start.13 = (f32[16,16,128]{2,1,0:T(8,128)S(1)}, f32[16,16,128]{2,1,0:T(8,128)}, u32[]{:S(2)}) copy-start(f32[16,16,128]{2,1,0:T(8,128)} %get-tuple-element.59) | copy-start | bytes 393220
  114.4 2.5 %copy-start.21 = (f32[16]{0:T(128)S(1)}, f32[16]{0:T(128)}, u32[]{:S(2)}) copy-start(f32[16]{0:T(128)} %param.20) | copy-start | bytes 196
  114.4 2.5 %copy-start.24 = (f32[4]{0:T(128)S(1)}, f32[4]{0:T(128)}, u32[]{:S(2)}) copy-start(f32[4]{0:T(128)} %pad.62.clone) | copy-start | bytes 52
  116.6 1.1 copy-start.3
  118.7 0.7 copy-start.25
  118.8 57.2 %copy-start.9 = (f32[4,16,16,128]{3,2,1,0:T(8,128)}, f32[4,16,16,128]{3,2,1,0:T(8,128)S(1)}, u32[]{:S(2)}) copy-start(f32[4,16,16,128]{3,2,1,0:T(8,128)S(1)} %multiply_add_fusion) | copy-start | bytes 1572868
Sparse Core Ops, SparseCore 0:
  120.4 55.5 reduce-scatter.1
where the time goes:
time: 184 us; the launch traced here: 183 us
  waiting for transfers between devices  64.8 us (35%)
  local copies, waits for them, and re-layouts  39.6 us (22%)
  starting transfers between devices  28.5 us (15%)
  blocking collectives  22.4 us (12%)
  between operations  14.6 us (8%)
  other arithmetic  11.8 us (6%)
    reduce_scatter x1, waiting for transfers between devices, per_device(): lax.psum_scatter(dense, 'ox', scatter_dimension=1, tiled=True)  55.7 us
    all_gather x1, blocking collectives, per_device(): whole = lax.all_gather(atm_flux, 'ox', axis=2, tiled=True)  22.4 us
    ppermute x6, starting transfers between devices, with_halo(): lax.ppermute(lax.slice_in_dim(block, block.shape[dim] - width, None, axis...  20.7 us
    slice x9, local copies, waits for them, and re-layouts, with_halo(): lax.slice_in_dim(block, block.shape[dim] - width, None, axis=dim)  11.5 us
    ppermute x6, waiting for transfers between devices, with_halo(): lax.ppermute(lax.slice_in_dim(block, 0, width, axis=dim), axis, backward)  7.92 us
    ppermute x6, starting transfers between devices, with_halo(): lax.ppermute(lax.slice_in_dim(block, 0, width, axis=dim), axis, backward)  7.72 us
    another operation x3, other arithmetic, advance(): pressure = jnp.cumsum(density, axis=0) - 0.5 * density  6.68 us
    ppermute x3, local copies, waits for them, and re-layouts, with_halo(): lax.ppermute(lax.slice_in_dim(block, 0, width, axis=dim), axis, backward)  6.43 us
  transfers between devices with their start and end apart: 13, of which 5 were waited for; matrix products, arithmetic and copies ran while one was open for 8% of the time, Pallas kernels for 0%

commit v1 on v0

--- a/solution.py
+++ b/solution.py
@@ -81,7 +81,12 @@
     tile_count = tile_slots.shape[0]
     refs_tile = tile_slots.shape[1]
     capacity = send_blocks.shape[1]
-    whole = lax.all_gather(atm_flux, "ox", axis=2, tiled=True)
+    ring = [atm_flux]
+    for hop in range(7):
+        ring.append(lax.ppermute(ring[-1], "ox", [(dev, (dev + 1) % 8) for dev in range(8)]))
+    whole = jnp.roll(
+        jnp.concatenate(ring[::-1], axis=2), (lax.axis_index("ox") + 1) * ring[0].shape[2], axis=2
+    )
     table = whole.reshape(flux_fields, blocks_here * owners, block_width)
     picks = table[:, row_targets(tile_slots, need_blocks, capacity, owners)]
     forcing = jnp.einsum("ftka,tkra->ftr", picks, remap_weights, preferred_element_type=jnp.float32)

time: 184 us -> 188 us (1.022)
  waiting for transfers between devices: 64.8 us -> 91.8 us
  blocking collectives: 22.4 us -> 0 us
  starting transfers between devices: 28.5 us -> 32.5 us
  local copies, waits for them, and re-layouts: 39.6 us -> 36.3 us
    ppermute x0 -> x7, waiting for transfers between devices: none -> 24.3 us  [per_device(): lax.ppermute(ring[-1], 'ox', [(dev, (dev + 1) % 8) for dev in range(8)])]
    all_gather x1 -> x0, blocking collectives: 22.4 us -> none  [per_device(): whole = lax.all_gather(atm_flux, 'ox', axis=2, tiled=True)]
    ppermute x0 -> x7, starting transfers between devices: none -> 7.22 us  [per_device(): lax.ppermute(ring[-1], 'ox', [(dev, (dev + 1) % 8) for dev in range(8)])]
    ppermute x6, starting transfers between devices: 20.7 us -> 17.5 us  [with_halo(): lax.ppermute(lax.slice_in_dim(block, block.shape[dim] - width, None, axis...]
    reduce_scatter x1, waiting for transfers between devices: 55.7 us -> 58.8 us  [per_device(): lax.psum_scatter(dense, 'ox', scatter_dimension=1, tiled=True)]
  transfers between devices with their start and end apart: 13 -> 20, of which waited for: 5 -> 10; matrix products, arithmetic and copies ran while one was open for 8% -> 11% of each run, Pallas kernels for 0% -> 0%
where the time goes in v1:
time: 188 us; the launch traced here: 187 us
  waiting for transfers between devices  91.8 us (49%)
  local copies, waits for them, and re-layouts  36.3 us (19%)
  starting transfers between devices  32.5 us (17%)
  between operations  14.8 us (8%)
  other arithmetic  10.5 us (6%)
    reduce_scatter x1, waiting for transfers between devices, per_device(): lax.psum_scatter(dense, 'ox', scatter_dimension=1, tiled=True)  58.8 us
    ppermute x7, waiting for transfers between devices, per_device(): lax.ppermute(ring[-1], 'ox', [(dev, (dev + 1) % 8) for dev in range(8)])  24.3 us
    ppermute x6, starting transfers between devices, with_halo(): lax.ppermute(lax.slice_in_dim(block, block.shape[dim] - width, None, axis...  17.5 us
    slice x9, local copies, waits for them, and re-layouts, with_halo(): lax.slice_in_dim(block, block.shape[dim] - width, None, axis=dim)  10.7 us
    ppermute x6, starting transfers between devices, with_halo(): lax.ppermute(lax.slice_in_dim(block, 0, width, axis=dim), axis, backward)  7.72 us
    ppermute x6, waiting for transfers between devices, with_halo(): lax.ppermute(lax.slice_in_dim(block, 0, width, axis=dim), axis, backward)  7.57 us
    ppermute x7, starting transfers between devices, per_device(): lax.ppermute(ring[-1], 'ox', [(dev, (dev + 1) % 8) for dev in range(8)])  7.22 us
    another operation x3, other arithmetic, advance(): pressure = jnp.cumsum(density, axis=0) - 0.5 * density  6.62 us
  transfers between devices with their start and end apart: 20, of which 10 were waited for; matrix products, arithmetic and copies ran while one was open for 11% of the time, Pallas kernels for 0%

profile of v1, /device:TPU:0, one launch (start us, length us, event | category | flops | bytes accessed | tf_op | source)
XLA Modules:
  0.0 187.2 jit_solution(10653873714528077479)
XLA Ops:
  7.2 3.0 %collective-permute-start.4 = (bf16[4,10,128]{2,0,1:T(4,128)(2,1)}, bf16[4,10,128]{2,0,1:T(4,128)(2,1)S(1)}, u32[]{:S(2)}, u32[]{:S(2)}) collective-permute-start(bf16[4,10,128]{2,0,1:T(4,128)(2,1)} %param.14), channel_id=1, source_target_pairs={{0,4},{4,8},{8,12},{12,16},{16,20},{20,24},{24,28},{28,0},{1,5},{5... | collective-permute-start | bytes 30728 | tf_op jit(solution)/shard_map/ppermute | solution.py:86
  10.2 1.1 fusion.83
  11.3 3.5 %collective-permute-start.1 = (f32[4,16,1,128]{3,2,1,0:T(1,128)S(1)}, f32[4,16,1,128]{3,2,1,0:T(1,128)S(1)}, u32[]{:S(2)}, u32[]{:S(2)}) collective-permute-start(f32[4,16,1,128]{3,2,1,0:T(1,128)S(1)} %get-tuple-element.76), channel_id=1, source_target_pairs={{0,4},{4,8},{8,12},{12,16},{16,20},{20,24},{24,28},{1,5},{5,9},{9,... | collective-permute-start | bytes 98312 | tf_op jit(solution)/shard_map/ppermute | solution.py:21
  14.8 1.3 collective-permute-start
  16.1 0.8 fusion.85
  16.9 1.7 slice_bitcast_fusion.5
  18.6 2.3 %fusion.84 = (f32[4,15,16,128]{3,2,1,0:T(8,128)}, f32[4,15,16,128]{3,2,1,0:T(8,128)}) fusion(f32[4,16,16,128]{3,2,1,0:T(8,128)} %param.18), kind=kLoop, calls=%fused_computation.180 | loop fusion | bytes 1966080 | tf_op jit(solution)/shard_map/slice | solution.py:41
  21.1 1.1 gather_fusion
  22.2 2.7 %collective-permute-start.5 = (bf16[4,10,128]{2,0,1:T(4,128)(2,1)S(1)}, bf16[4,10,128]{2,0,1:T(4,128)(2,1)S(1)}, u32[]{:S(2)}, u32[]{:S(2)}) collective-permute-start(bf16[4,10,128]{2,0,1:T(4,128)(2,1)S(1)} %collective-permute-done.4), channel_id=1, source_target_pairs={{0,4},{4,8},{8,12},{12,16},{16,20},{20,24},{24,28},{28,0},{1,5},{5... | collective-permute-start | bytes 30728 | tf_op jit(solution)/shard_map/ppermute | solution.py:86
  25.0 3.6 %collective-permute-done.5 = bf16[4,10,128]{2,0,1:T(4,128)(2,1)S(1)} collective-permute-done((bf16[4,10,128]{2,0,1:T(4,128)(2,1)S(1)}, bf16[4,10,128]{2,0,1:T(4,128)(2,1)S(1)}, u32[]{:S(2)}, u32[]{:S(2)}) %collective-permute-start.5) | collective-permute-done | bytes 10272 | tf_op jit(solution)/shard_map/ppermute | solution.py:86
  28.7 6.3 %collective-permute-done.6 = bf16[4,10,128]{2,0,1:T(4,128)(2,1)S(1)} collective-permute-done((bf16[4,10,128]{2,0,1:T(4,128)(2,1)S(1)}, bf16[4,10,128]{2,0,1:T(4,128)(2,1)S(1)}, u32[]{:S(2)}, u32[]{:S(2)}) %collective-permute-start.6) | collective-permute-done | bytes 10272 | tf_op jit(solution)/shard_map/ppermute | solution.py:86
  35.2 1.2 fusion.76
  36.4 1.6 copy.144
  38.0 0.5 copy.142
  38.5 1.3 collective-permute-start.2
  39.8 3.0 %collective-permute-start.3 = (f32[4,16,18,1]{2,1,3,0:T(8,128)S(1)}, f32[4,16,18,1]{2,1,3,0:T(8,128)S(1)}, u32[]{:S(2)}, u32[]{:S(2)}) collective-permute-start(f32[4,16,18,1]{2,1,3,0:T(8,128)S(1)} %copy.144), channel_id=1, source_target_pairs={{0,1},{1,2},{2,3},{4,5},{5,6},{6,7},{8,9},{9,10},{10,11},{12,13},{... | collective-permute-start | bytes 13832 | tf_op jit(solution)/shard_map/ppermute | solution.py:21
  42.9 0.7 eq.21
  43.6 0.6 pad.62.clone
  44.1 0.5 copy.145
  44.7 1.4 copy.143
  46.1 1.5 collective-permute-start.8
  47.6 2.2 %reduce-window_subtract_fusion.2 = f32[16,18,130]{2,1,0:T(8,128)S(1)} fusion(f32[4,16,18,1]{3,2,1,0:T(8,128)} %copy.143, f32[4,16,1,128]{3,2,1,0:T(1,128)S(1)} %collective-permute-done, f32[4,16,16,128]{3,2,1,0:T(8,128)S(1)} %copy-done.2, f32[4,16,1,128]{3,2,1,0:T(1,128)S(1)} %collective-permute-done.1, f32[4,16,18,1]{3,2,1,0:T(8,128)S(1)} %copy.145), kind=kOutput, calls=%fused_computation.4 | output fusion | flops 1460160 | bytes 748800 | tf_op jit(solution)/shard_map/jit(cumsum)/reduce_window_sum | solution.py:44
  49.8 2.8 %collective-permute-done.8 = bf16[4,10,128]{2,0,1:T(4,128)(2,1)S(1)} collective-permute-done((bf16[4,10,128]{2,0,1:T(4,128)(2,1)S(1)}, bf16[4,10,128]{2,0,1:T(4,128)(2,1)S(1)}, u32[]{:S(2)}, u32[]{:S(2)}) %collective-permute-start.8) | collective-permute-done | bytes 10272 | tf_op jit(solution)/shard_map/ppermute | solution.py:86
  52.7 6.2 %collective-permute-done.9 = bf16[4,10,128]{2,0,1:T(4,128)(2,1)S(1)} collective-permute-done((bf16[4,10,128]{2,0,1:T(4,128)(2,1)S(1)}, bf16[4,10,128]{2,0,1:T(4,128)(2,1)S(1)}, u32[]{:S(2)}, u32[]{:S(2)}) %collective-permute-start.9) | collective-permute-done | bytes 10272 | tf_op jit(solution)/shard_map/ppermute | solution.py:86
  59.0 0.9 fusion.3
  59.9 5.4 %collective-permute-done.10 = bf16[4,10,128]{2,0,1:T(4,128)(2,1)S(1)} collective-permute-done((bf16[4,10,128]{2,0,1:T(4,128)(2,1)S(1)}, bf16[4,10,128]{2,0,1:T(4,128)(2,1)S(1)}, u32[]{:S(2)}, u32[]{:S(2)}) %collective-permute-start.10) | collective-permute-done | bytes 10272 | tf_op jit(solution)/shard_map/ppermute | solution.py:86
  65.7 0.6 gather_fusion.1
  66.3 0.6 convolution_bitcast_fusion
  67.1 0.9 fusion.81
  68.0 1.3 collective-permute-start.12
  69.2 1.3 collective-permute-start.11
  70.5 0.7 slice_bitcast_fusion.3
  71.3 3.8 %collective-permute-done.11 = f32[4,16,1,128]{3,2,1,0:T(1,128)S(1)} collective-permute-done((f32[4,16,1,128]{3,2,1,0:T(1,128)S(1)}, f32[4,16,1,128]{3,2,1,0:T(1,128)S(1)}, u32[]{:S(2)}, u32[]{:S(2)}) %collective-permute-start.11) | collective-permute-done | bytes 32800 | tf_op jit(solution)/shard_map/ppermute | solution.py:24
  75.2 1.2 fusion.75
  76.4 2.2 %copy.156 = f32[4,16,18,1]{2,1,3,0:T(8,128)} copy(f32[4,16,18,1]{3,2,1,0:T(8,128)} %get-tuple-element.54) | data formatting | bytes 9216 | tf_op jit(solution)/shard_map/slice | solution.py:22
  78.6 1.1 copy.154
  79.6 1.3 collective-permute-start.13
  80.9 3.6 %collective-permute-start.14 = (f32[4,16,18,1]{2,1,3,0:T(8,128)}, f32[4,16,18,1]{2,1,3,0:T(8,128)}, u32[]{:S(2)}, u32[]{:S(2)}) collective-permute-start(f32[4,16,18,1]{2,1,3,0:T(8,128)} %copy.156), channel_id=1, source_target_pairs={{0,1},{1,2},{2,3},{4,5},{5,6},{6,7},{8,9},{9,10},{10,11},{12,13},{... | collective-permute-start | bytes 13832 | tf_op jit(solution)/shard_map/ppermute | solution.py:21
  84.6 0.6 collective-permute-done.14
  85.1 1.3 copy.157
  86.4 2.1 %copy.155 = f32[4,16,18,1]{3,2,1,0:T(8,128)} copy(f32[4,16,18,1]{2,1,3,0:T(8,128)} %collective-permute-done.13) | data formatting | bytes 9216 | tf_op jit(solution)/shard_map/ppermute | solution.py:24
  88.6 2.2 %reduce-window_subtract_fusion.1 = f32[16,18,130]{2,1,0:T(8,128)S(1)} fusion(f32[4,16,18,1]{3,2,1,0:T(8,128)} %copy.155, f32[4,16,1,128]{3,2,1,0:T(1,128)S(1)} %collective-permute-done.11, f32[4,16,16,128]{3,2,1,0:T(8,128)S(1)} %multiply_add_fusion.2, f32[4,16,1,128]{3,2,1,0:T(1,128)S(1)} %collective-permute-done.12, f32[4,16,18,1]{3,2,1,0:T(8,128)S(1)} %copy.157), kind=kOutput, calls=%fused_computation.3 | output fusion | flops 1460160 | bytes 748800 | tf_op jit(solution)/shard_map/jit(cumsum)/reduce_window_sum | solution.py:44
  91.1 0.9 copy-done.5
  92.0 0.9 fusion.7
  93.0 0.9 fusion.78
  93.9 1.6 collective-permute-start.16
  95.5 1.3 collective-permute-start.15
  96.8 0.7 slice_bitcast_fusion.1
  97.5 3.8 %collective-permute-done.15 = f32[4,16,1,128]{3,2,1,0:T(1,128)S(1)} collective-permute-done((f32[4,16,1,128]{3,2,1,0:T(1,128)S(1)}, f32[4,16,1,128]{3,2,1,0:T(1,128)S(1)}, u32[]{:S(2)}, u32[]{:S(2)}) %collective-permute-start.15) | collective-permute-done | bytes 32800 | tf_op jit(solution)/shard_map/ppermute | solution.py:24
  101.4 1.2 fusion.74
  102.6 2.2 %copy.162 = f32[4,16,18,1]{2,1,3,0:T(8,128)} copy(f32[4,16,18,1]{3,2,1,0:T(8,128)} %get-tuple-element.52) | data formatting | bytes 9216 | tf_op jit(solution)/shard_map/slice | solution.py:22
  104.8 1.1 copy.160
  105.9 1.3 collective-permute-start.17
  107.2 4.5 %collective-permute-start.18 = (f32[4,16,18,1]{2,1,3,0:T(8,128)}, f32[4,16,18,1]{2,1,3,0:T(8,128)}, u32[]{:S(2)}, u32[]{:S(2)}) collective-permute-start(f32[4,16,18,1]{2,1,3,0:T(8,128)} %copy.162), channel_id=1, source_target_pairs={{0,1},{1,2},{2,3},{4,5},{5,6},{6,7},{8,9},{9,10},{10,11},{12,13},{... | collective-permute-start | bytes 13832 | tf_op jit(solution)/shard_map/ppermute | solution.py:21
  111.7 0.6 collective-permute-done.18
  112.2 1.3 copy.163
  113.5 2.1 %copy.161 = f32[4,16,18,1]{3,2,1,0:T(8,128)} copy(f32[4,16,18,1]{2,1,3,0:T(8,128)} %collective-permute-done.17) | data formatting | bytes 9216 | tf_op jit(solution)/shard_map/ppermute | solution.py:24
  115.7 2.2 %reduce-window_subtract_fusion = f32[16,18,130]{2,1,0:T(8,128)S(1)} fusion(f32[4,16,18,1]{3,2,1,0:T(8,128)} %copy.161, f32[4,16,1,128]{3,2,1,0:T(1,128)S(1)} %collective-permute-done.15, f32[4,16,16,128]{3,2,1,0:T(8,128)S(1)} %multiply_add_fusion.1, f32[4,16,1,128]{3,2,1,0:T(1,128)S(1)} %collective-permute-done.16, f32[4,16,18,1]{3,2,1,0:T(8,128)S(1)} %copy.163), kind=kOutput, calls=%fused_computation.2 | output fusion | flops 1460160 | bytes 748800 | tf_op jit(solution)/shard_map/jit(cumsum)/reduce_window_sum | solution.py:44
  118.1 0.9 copy-done.4
  119.0 0.9 fusion.11
  120.1 0.4 fusion.58
  120.6 0.3 fusion.51
  120.9 0.6 reshape.143
  121.6 58.8 %reduce-scatter.2.cloned.1.call-done = f32[10,128]{1,0:T(8,128)} async-done(((f32[10,1024]{1,0:T(8,128)}), f32[10,128]{1,0:T(8,128)}) %reduce-scatter.2.cloned.1.call-update) | async-done | bytes 5136 | tf_op jit(solution)/shard_map/reduce_scatter | solution.py:112
  (135 shorter events, 2.4 us)
Async XLA Ops:
  7.2 59.1 %copy-start = (bf16[16,3,128,128]{3,2,1,0:T(8,128)(2,1)S(1)}, bf16[16,3,128,128]{3,2,1,0:T(8,128)(2,1)}, u32[]{:S(2)}) copy-start(bf16[16,3,128,128]{3,2,1,0:T(8,128)(2,1)} %param.15) | copy-start | bytes 4718596
  7.2 13.7 %copy-start.36 = (s32[16,3]{0,1:T(4,128)S(1)}, s32[16,3]{0,1:T(4,128)}, u32[]{:S(2)}) copy-start(s32[16,3]{0,1:T(4,128)} %param.16) | copy-start | bytes 580
  7.2 13.9 %copy-start.1 = (s32[8,3]{0,1:T(4,128)S(1)}, s32[8,3]{0,1:T(4,128)}, u32[]{:S(2)}) copy-start(s32[8,3]{0,1:T(4,128)} %param.17) | copy-start | bytes 292
  7.2 173.1 %reduce-scatter.2.cloned.1.call-start = ((), (), s32[]{:S(2)}) async-start(), calls=%async_computation.1 | async-start | bytes 73728 | tf_op jit(solution)/shard_map/reduce_scatter | solution.py:112
  7.2 15.0 %collective-permute-start.4 = (bf16[4,10,128]{2,0,1:T(4,128)(2,1)}, bf16[4,10,128]{2,0,1:T(4,128)(2,1)S(1)}, u32[]{:S(2)}, u32[]{:S(2)}) collective-permute-start(bf16[4,10,128]{2,0,1:T(4,128)(2,1)} %param.14), channel_id=1, source_target_pairs={{0,4},{4,8},{8,12},{12,16},{16,20},{20,24},{24,28},{28,0},{1,5},{5... | collective-permute-start | bytes 30728 | tf_op jit(solution)/shard_map/ppermute | solution.py:86
  11.3 23.7 %collective-permute-start.1 = (f32[4,16,1,128]{3,2,1,0:T(1,128)S(1)}, f32[4,16,1,128]{3,2,1,0:T(1,128)S(1)}, u32[]{:S(2)}, u32[]{:S(2)}) collective-permute-start(f32[4,16,1,128]{3,2,1,0:T(1,128)S(1)} %get-tuple-element.76), channel_id=1, source_target_pairs={{0,4},{4,8},{8,12},{12,16},{16,20},{20,24},{24,28},{1,5},{5,9},{9,... | collective-permute-start | bytes 98312 | tf_op jit(solution)/shard_map/ppermute | solution.py:21
  14.8 20.3 %collective-permute-start = (f32[4,16,1,128]{3,2,1,0:T(1,128)S(1)}, f32[4,16,1,128]{3,2,1,0:T(1,128)S(1)}, u32[]{:S(2)}, u32[]{:S(2)}) collective-permute-start(f32[4,16,1,128]{3,2,1,0:T(1,128)S(1)} %get-tuple-element.77), channel_id=1, source_target_pairs={{4,0},{8,4},{12,8},{16,12},{20,16},{24,20},{28,24},{5,1},{9,5},{13... | collective-permute-start | bytes 98312 | tf_op jit(solution)/shard_map/ppermute | solution.py:24
  21.0 14.0 %copy-start.2 = (f32[4,16,16,128]{3,2,1,0:T(8,128)S(1)}, f32[4,16,16,128]{3,2,1,0:T(8,128)}, u32[]{:S(2)}) copy-start(f32[4,16,16,128]{3,2,1,0:T(8,128)} %param.18) | copy-start | bytes 1572868
  22.2 12.8 %copy-start.18 = (bf16[4,10,128]{2,0,1:T(4,128)(2,1)}, bf16[4,10,128]{2,0,1:T(4,128)(2,1)S(1)}, u32[]{:S(2)}) copy-start(bf16[4,10,128]{2,0,1:T(4,128)(2,1)S(1)} %collective-permute-done.4) | copy-start | bytes 30724
  22.2 6.4 %collective-permute-start.5 = (bf16[4,10,128]{2,0,1:T(4,128)(2,1)S(1)}, bf16[4,10,128]{2,0,1:T(4,128)(2,1)S(1)}, u32[]{:S(2)}, u32[]{:S(2)}) collective-permute-start(bf16[4,10,128]{2,0,1:T(4,128)(2,1)S(1)} %collective-permute-done.4), channel_id=1, source_target_pairs={{0,4},{4,8},{8,12},{12,16},{16,20},{20,24},{24,28},{28,0},{1,5},{5... | collective-permute-start | bytes 30728 | tf_op jit(solution)/shard_map/ppermute | solution.py:86
  28.7 6.4 %copy-start.20 = (bf16[4,10,128]{2,0,1:T(4,128)(2,1)}, bf16[4,10,128]{2,0,1:T(4,128)(2,1)S(1)}, u32[]{:S(2)}) copy-start(bf16[4,10,128]{2,0,1:T(4,128)(2,1)S(1)} %collective-permute-done.5) | copy-start | bytes 30724
  28.7 6.4 %collective-permute-start.6 = (bf16[4,10,128]{2,0,1:T(4,128)(2,1)S(1)}, bf16[4,10,128]{2,0,1:T(4,128)(2,1)S(1)}, u32[]{:S(2)}, u32[]{:S(2)}) collective-permute-start(bf16[4,10,128]{2,0,1:T(4,128)(2,1)S(1)} %collective-permute-done.5), channel_id=1, source_target_pairs={{0,4},{4,8},{8,12},{12,16},{16,20},{20,24},{24,28},{28,0},{1,5},{5... | collective-permute-start | bytes 30728 | tf_op jit(solution)/shard_map/ppermute | solution.py:86
  35.0 1.4 copy-start.22
  35.0 11.1 %collective-permute-start.7 = (bf16[4,10,128]{2,0,1:T(4,128)(2,1)S(1)}, bf16[4,10,128]{2,0,1:T(4,128)(2,1)S(1)}, u32[]{:S(2)}, u32[]{:S(2)}) collective-permute-start(bf16[4,10,128]{2,0,1:T(4,128)(2,1)S(1)} %collective-permute-done.6), channel_id=1, source_target_pairs={{0,4},{4,8},{8,12},{12,16},{16,20},{20,24},{24,28},{28,0},{1,5},{5... | collective-permute-start | bytes 30728 | tf_op jit(solution)/shard_map/ppermute | solution.py:86
  36.4 6.5 %copy-start.26 = (s32[16,128]{1,0:T(8,128)S(1)}, s32[16,128]{1,0:T(8,128)}, u32[]{:S(2)}) copy-start(s32[16,128]{1,0:T(8,128)} %param.19) | copy-start | bytes 24580
  38.5 6.2 %collective-permute-start.2 = (f32[4,16,18,1]{2,1,3,0:T(8,128)S(1)}, f32[4,16,18,1]{2,1,3,0:T(8,128)S(1)}, u32[]{:S(2)}, u32[]{:S(2)}) collective-permute-start(f32[4,16,18,1]{2,1,3,0:T(8,128)S(1)} %copy.142), channel_id=1, source_target_pairs={{1,0},{2,1},{3,2},{5,4},{6,5},{7,6},{9,8},{10,9},{11,10},{13,12},{... | collective-permute-start | bytes 13832 | tf_op jit(solution)/shard_map/ppermute | solution.py:24
  39.8 4.4 %collective-permute-start.3 = (f32[4,16,18,1]{2,1,3,0:T(8,128)S(1)}, f32[4,16,18,1]{2,1,3,0:T(8,128)S(1)}, u32[]{:S(2)}, u32[]{:S(2)}) collective-permute-start(f32[4,16,18,1]{2,1,3,0:T(8,128)S(1)} %copy.144), channel_id=1, source_target_pairs={{0,1},{1,2},{2,3},{4,5},{5,6},{6,7},{8,9},{9,10},{10,11},{12,13},{... | collective-permute-start | bytes 13832 | tf_op jit(solution)/shard_map/ppermute | solution.py:21
  42.8 9.7 %copy-start.27 = (f32[128]{0:T(128)}, f32[128]{0:T(128)S(1)}, u32[]{:S(2)}) copy-start(f32[128]{0:T(128)S(1)} %get-tuple-element.83) | copy-start | bytes 1540
  46.1 12.9 %copy-start.6 = (f32[4,15,16,128]{3,2,1,0:T(8,128)S(1)}, f32[4,15,16,128]{3,2,1,0:T(8,128)}, u32[]{:S(2)}) copy-start(f32[4,15,16,128]{3,2,1,0:T(8,128)} %get-tuple-element.78) | copy-start | bytes 1474564
  46.1 12.9 %copy-start.7 = (f32[4,15,16,128]{3,2,1,0:T(8,128)S(1)}, f32[4,15,16,128]{3,2,1,0:T(8,128)}, u32[]{:S(2)}) copy-start(f32[4,15,16,128]{3,2,1,0:T(8,128)} %get-tuple-element.79) | copy-start | bytes 1474564
  46.1 12.9 %copy-start.11 = (f32[16,16,128]{2,1,0:T(8,128)S(1)}, f32[16,16,128]{2,1,0:T(8,128)}, u32[]{:S(2)}) copy-start(f32[16,16,128]{2,1,0:T(8,128)} %get-tuple-element.74) | copy-start | bytes 393220
  46.1 12.9 %copy-start.12 = (f32[16,16,128]{2,1,0:T(8,128)S(1)}, f32[16,16,128]{2,1,0:T(8,128)}, u32[]{:S(2)}) copy-start(f32[16,16,128]{2,1,0:T(8,128)} %get-tuple-element.75) | copy-start | bytes 393220
  46.1 12.9 %copy-start.29 = (f32[16]{0:T(128)S(1)}, f32[16]{0:T(128)}, u32[]{:S(2)}) copy-start(f32[16]{0:T(128)} %param.20) | copy-start | bytes 196
  46.1 12.9 %copy-start.32 = (f32[4]{0:T(128)S(1)}, f32[4]{0:T(128)}, u32[]{:S(2)}) copy-start(f32[4]{0:T(128)} %pad.62.clone) | copy-start | bytes 52
  46.1 3.7 %copy-start.24 = (bf16[4,10,128]{2,0,1:T(4,128)(2,1)}, bf16[4,10,128]{2,0,1:T(4,128)(2,1)S(1)}, u32[]{:S(2)}) copy-start(bf16[4,10,128]{2,0,1:T(4,128)(2,1)S(1)} %collective-permute-done.7) | copy-start | bytes 30724
  46.1 6.4 %collective-permute-start.8 = (bf16[4,10,128]{2,0,1:T(4,128)(2,1)S(1)}, bf16[4,10,128]{2,0,1:T(4,128)(2,1)S(1)}, u32[]{:S(2)}, u32[]{:S(2)}) collective-permute-start(bf16[4,10,128]{2,0,1:T(4,128)(2,1)S(1)} %collective-permute-done.7), channel_id=1, source_target_pairs={{0,4},{4,8},{8,12},{12,16},{16,20},{20,24},{24,28},{28,0},{1,5},{5... | collective-permute-start | bytes 30728 | tf_op jit(solution)/shard_map/ppermute | solution.py:86
  49.8 9.2 %copy-start.3 = (f32[4,16,18,1]{3,2,1,0:T(8,128)S(1)}, f32[4,16,18,1]{3,2,1,0:T(8,128)}, u32[]{:S(2)}) copy-start(f32[4,16,18,1]{3,2,1,0:T(8,128)} %copy.143) | copy-start | bytes 13828
  52.5 6.4 %collective-permute-start.9 = (bf16[4,10,128]{2,0,1:T(4,128)(2,1)S(1)}, bf16[4,10,128]{2,0,1:T(4,128)(2,1)S(1)}, u32[]{:S(2)}, u32[]{:S(2)}) collective-permute-start(bf16[4,10,128]{2,0,1:T(4,128)(2,1)S(1)} %collective-permute-done.8), channel_id=1, source_target_pairs={{0,4},{4,8},{8,12},{12,16},{16,20},{20,24},{24,28},{28,0},{1,5},{5... | collective-permute-start | bytes 30728 | tf_op jit(solution)/shard_map/ppermute | solution.py:86
  58.9 6.4 %collective-permute-start.10 = (bf16[4,10,128]{2,0,1:T(4,128)(2,1)S(1)}, bf16[4,10,128]{2,0,1:T(4,128)(2,1)S(1)}, u32[]{:S(2)}, u32[]{:S(2)}) collective-permute-start(bf16[4,10,128]{2,0,1:T(4,128)(2,1)S(1)} %collective-permute-done.9), channel_id=1, source_target_pairs={{0,4},{4,8},{8,12},{12,16},{16,20},{20,24},{24,28},{28,0},{1,5},{5... | collective-permute-start | bytes 30728 | tf_op jit(solution)/shard_map/ppermute | solution.py:86
  59.0 6.4 %copy-start.25 = (bf16[4,10,128]{2,0,1:T(4,128)(2,1)S(1)}, bf16[4,10,128]{2,0,1:T(4,128)(2,1)}, u32[]{:S(2)}) copy-start(bf16[4,10,128]{2,0,1:T(4,128)(2,1)} %copy-done.24) | copy-start | bytes 30724
  59.0 6.4 %copy-start.23 = (bf16[4,10,128]{2,0,1:T(4,128)(2,1)S(1)}, bf16[4,10,128]{2,0,1:T(4,128)(2,1)}, u32[]{:S(2)}) copy-start(bf16[4,10,128]{2,0,1:T(4,128)(2,1)} %copy-done.22) | copy-start | bytes 30724
  59.0 6.4 %copy-start.21 = (bf16[4,10,128]{2,0,1:T(4,128)(2,1)S(1)}, bf16[4,10,128]{2,0,1:T(4,128)(2,1)}, u32[]{:S(2)}) copy-start(bf16[4,10,128]{2,0,1:T(4,128)(2,1)} %copy-done.20) | copy-start | bytes 30724
  59.0 6.4 %copy-start.19 = (bf16[4,10,128]{2,0,1:T(4,128)(2,1)S(1)}, bf16[4,10,128]{2,0,1:T(4,128)(2,1)}, u32[]{:S(2)}) copy-start(bf16[4,10,128]{2,0,1:T(4,128)(2,1)} %copy-done.18) | copy-start | bytes 30724
  59.0 6.4 %copy-start.17 = (bf16[4,10,128]{2,0,1:T(4,128)(2,1)S(1)}, bf16[4,10,128]{2,0,1:T(4,128)(2,1)}, u32[]{:S(2)}) copy-start(bf16[4,10,128]{2,0,1:T(4,128)(2,1)} %param.14) | copy-start | bytes 30724
  68.0 3.3 %collective-permute-start.12 = (f32[4,16,1,128]{3,2,1,0:T(1,128)S(1)}, f32[4,16,1,128]{3,2,1,0:T(1,128)S(1)}, u32[]{:S(2)}, u32[]{:S(2)}) collective-permute-start(f32[4,16,1,128]{3,2,1,0:T(1,128)S(1)} %get-tuple-element.68), channel_id=1, source_target_pairs={{0,4},{4,8},{8,12},{12,16},{16,20},{20,24},{24,28},{1,5},{5,9},{9,... | collective-permute-start | bytes 98312 | tf_op jit(solution)/shard_map/ppermute | solution.py:21
  69.2 5.8 %collective-permute-start.11 = (f32[4,16,1,128]{3,2,1,0:T(1,128)S(1)}, f32[4,16,1,128]{3,2,1,0:T(1,128)S(1)}, u32[]{:S(2)}, u32[]{:S(2)}) collective-permute-start(f32[4,16,1,128]{3,2,1,0:T(1,128)S(1)} %get-tuple-element.69), channel_id=1, source_target_pairs={{4,0},{8,4},{12,8},{16,12},{20,16},{24,20},{28,24},{5,1},{9,5},{13... | collective-permute-start | bytes 98312 | tf_op jit(solution)/shard_map/ppermute | solution.py:24
  79.6 6.8 %collective-permute-start.13 = (f32[4,16,18,1]{2,1,3,0:T(8,128)}, f32[4,16,18,1]{2,1,3,0:T(8,128)}, u32[]{:S(2)}, u32[]{:S(2)}) collective-permute-start(f32[4,16,18,1]{2,1,3,0:T(8,128)} %copy.154), channel_id=1, source_target_pairs={{1,0},{2,1},{3,2},{5,4},{6,5},{7,6},{9,8},{10,9},{11,10},{13,12},{... | collective-permute-start | bytes 13832 | tf_op jit(solution)/shard_map/ppermute | solution.py:24
  80.9 4.2 %collective-permute-start.14 = (f32[4,16,18,1]{2,1,3,0:T(8,128)}, f32[4,16,18,1]{2,1,3,0:T(8,128)}, u32[]{:S(2)}, u32[]{:S(2)}) collective-permute-start(f32[4,16,18,1]{2,1,3,0:T(8,128)} %copy.156), channel_id=1, source_target_pairs={{0,1},{1,2},{2,3},{4,5},{5,6},{6,7},{8,9},{9,10},{10,11},{12,13},{... | collective-permute-start | bytes 13832 | tf_op jit(solution)/shard_map/ppermute | solution.py:21
  88.6 2.3 %copy-start.28 = (f32[128]{0:T(128)S(1)}, f32[128]{0:T(128)}, u32[]{:S(2)}) copy-start(f32[128]{0:T(128)} %copy-done.27) | copy-start | bytes 1540
  88.6 2.5 %copy-start.9 = (f32[4,15,16,128]{3,2,1,0:T(8,128)S(1)}, f32[4,15,16,128]{3,2,1,0:T(8,128)}, u32[]{:S(2)}) copy-start(f32[4,15,16,128]{3,2,1,0:T(8,128)} %get-tuple-element.71) | copy-start | bytes 1474564
  88.6 2.5 %copy-start.15 = (f32[16,16,128]{2,1,0:T(8,128)S(1)}, f32[16,16,128]{2,1,0:T(8,128)}, u32[]{:S(2)}) copy-start(f32[16,16,128]{2,1,0:T(8,128)} %get-tuple-element.66) | copy-start | bytes 393220
  88.6 2.5 %copy-start.16 = (f32[16,16,128]{2,1,0:T(8,128)S(1)}, f32[16,16,128]{2,1,0:T(8,128)}, u32[]{:S(2)}) copy-start(f32[16,16,128]{2,1,0:T(8,128)} %get-tuple-element.67) | copy-start | bytes 393220
  88.6 2.5 %copy-start.30 = (f32[16]{0:T(128)S(1)}, f32[16]{0:T(128)}, u32[]{:S(2)}) copy-start(f32[16]{0:T(128)} %param.20) | copy-start | bytes 196
  88.6 2.5 %copy-start.33 = (f32[4]{0:T(128)S(1)}, f32[4]{0:T(128)}, u32[]{:S(2)}) copy-start(f32[4]{0:T(128)} %pad.62.clone) | copy-start | bytes 52
  90.8 1.1 copy-start.5
  93.9 3.6 %collective-permute-start.16 = (f32[4,16,1,128]{3,2,1,0:T(1,128)S(1)}, f32[4,16,1,128]{3,2,1,0:T(1,128)S(1)}, u32[]{:S(2)}, u32[]{:S(2)}) collective-permute-start(f32[4,16,1,128]{3,2,1,0:T(1,128)S(1)} %get-tuple-element.60), channel_id=1, source_target_pairs={{0,4},{4,8},{8,12},{12,16},{16,20},{20,24},{24,28},{1,5},{5,9},{9,... | collective-permute-start | bytes 98312 | tf_op jit(solution)/shard_map/ppermute | solution.py:21
  95.5 5.8 %collective-permute-start.15 = (f32[4,16,1,128]{3,2,1,0:T(1,128)S(1)}, f32[4,16,1,128]{3,2,1,0:T(1,128)S(1)}, u32[]{:S(2)}, u32[]{:S(2)}) collective-permute-start(f32[4,16,1,128]{3,2,1,0:T(1,128)S(1)} %get-tuple-element.61), channel_id=1, source_target_pairs={{4,0},{8,4},{12,8},{16,12},{20,16},{24,20},{28,24},{5,1},{9,5},{13... | collective-permute-start | bytes 98312 | tf_op jit(solution)/shard_map/ppermute | solution.py:24
  105.9 7.6 %collective-permute-start.17 = (f32[4,16,18,1]{2,1,3,0:T(8,128)}, f32[4,16,18,1]{2,1,3,0:T(8,128)}, u32[]{:S(2)}, u32[]{:S(2)}) collective-permute-start(f32[4,16,18,1]{2,1,3,0:T(8,128)} %copy.160), channel_id=1, source_target_pairs={{1,0},{2,1},{3,2},{5,4},{6,5},{7,6},{9,8},{10,9},{11,10},{13,12},{... | collective-permute-start | bytes 13832 | tf_op jit(solution)/shard_map/ppermute | solution.py:24
  107.2 5.1 %collective-permute-start.18 = (f32[4,16,18,1]{2,1,3,0:T(8,128)}, f32[4,16,18,1]{2,1,3,0:T(8,128)}, u32[]{:S(2)}, u32[]{:S(2)}) collective-permute-start(f32[4,16,18,1]{2,1,3,0:T(8,128)} %copy.162), channel_id=1, source_target_pairs={{0,1},{1,2},{2,3},{4,5},{5,6},{6,7},{8,9},{9,10},{10,11},{12,13},{... | collective-permute-start | bytes 13832 | tf_op jit(solution)/shard_map/ppermute | solution.py:21
  115.6 2.4 %copy-start.8 = (f32[4,15,16,128]{3,2,1,0:T(8,128)S(1)}, f32[4,15,16,128]{3,2,1,0:T(8,128)}, u32[]{:S(2)}) copy-start(f32[4,15,16,128]{3,2,1,0:T(8,128)} %get-tuple-element.63) | copy-start | bytes 1474564
  115.6 2.4 %copy-start.13 = (f32[16,16,128]{2,1,0:T(8,128)S(1)}, f32[16,16,128]{2,1,0:T(8,128)}, u32[]{:S(2)}) copy-start(f32[16,16,128]{2,1,0:T(8,128)} %get-tuple-element.58) | copy-start | bytes 393220
  115.6 2.5 %copy-start.14 = (f32[16,16,128]{2,1,0:T(8,128)S(1)}, f32[16,16,128]{2,1,0:T(8,128)}, u32[]{:S(2)}) copy-start(f32[16,16,128]{2,1,0:T(8,128)} %get-tuple-element.59) | copy-start | bytes 393220
  115.7 2.5 %copy-start.31 = (f32[16]{0:T(128)S(1)}, f32[16]{0:T(128)}, u32[]{:S(2)}) copy-start(f32[16]{0:T(128)} %param.20) | copy-start | bytes 196
  115.7 2.5 %copy-start.34 = (f32[4]{0:T(128)S(1)}, f32[4]{0:T(128)}, u32[]{:S(2)}) copy-start(f32[4]{0:T(128)} %pad.62.clone) | copy-start | bytes 52
  117.9 1.1 copy-start.4
  119.9 0.7 copy-start.35
  120.0 60.3 %copy-start.10 = (f32[4,16,16,128]{3,2,1,0:T(8,128)}, f32[4,16,16,128]{3,2,1,0:T(8,128)S(1)}, u32[]{:S(2)}) copy-start(f32[4,16,16,128]{3,2,1,0:T(8,128)S(1)} %multiply_add_fusion) | copy-start | bytes 1572868
Sparse Core Ops, SparseCore 0:
  121.7 58.5 reduce-scatter.1
